TPU v7x, 256 devices: a whole 4x4x8 slice. The times are simulated.
256 devices in a mesh: link: 64 (over x, z, core), col: 4 (over y).
Axes of the slice: x: 4, y: 4, z: 8, core: 2. Of those that a mesh axis runs over, the one named last changes fastest.
Arguments:
- values: bfloat16 [1024, 16, 128], P('link'), may hold values from -6 to 6
- tiles: int32 [1024, 16], P('link'), may hold values from 0 to 127, all different within a row
- barrier: float32 [1024], P('link'), may hold values from 0.5 to 2
- slack: float32 [16384], replicated, may hold values from 0.5 to 2
- order: int32 [128], replicated, may hold values from 0 to 127, each once
Outputs:
- factored: float32 [16384, 16384], P('link', 'col')
Inputs may be any that keep to these rules, and one draw needn't show every extreme that they name: `tiles`: each commodity's 16 tile numbers are distinct, and every tile is named by some commodity. `order`: each tile number appears once.
All inputs are finite; a program needn't handle non-finite values.
Results may differ from a plain program's by a relative error of at most 0.0038.
Values may be sent and summed in bfloat16 or wider, within the bound.
No kernel may reach another device: no remote copies, remote signals or barrier semaphores. Data moves between devices by JAX's collectives and lax.ppermute only.
A program may use at most 64 MiB of HBM per device.

v0:
```python
import jax
import jax.numpy as jnp
from jax import lax
from jax.sharding import PartitionSpec as P

PANEL = 128
SUB = 8
HI = lax.Precision.HIGHEST


def densify(vals, ids, targets):
    groups, rows, tile_len = vals.shape
    tpc = rows // SUB
    nt = targets.shape[0]
    hits = (ids[:, None, :] == targets[None, :, None]).astype(jnp.bfloat16)
    own = (jnp.arange(SUB)[:, None] == jnp.arange(rows)[None, :] // tpc).astype(jnp.bfloat16)
    spread = (hits[:, :, None, :] * own[None, None, :, :]).reshape(groups, nt * SUB, rows)
    dense_out = lax.dot_general(
        spread, vals, (((2,), (1,)), ((0,), (0,))), preferred_element_type=jnp.float32,
    )
    dense_out = dense_out.astype(jnp.bfloat16).reshape(groups, nt, SUB, tile_len)
    return dense_out.transpose(0, 2, 1, 3).reshape(groups * SUB, nt * tile_len)


def gather_links(part, link_devs):
    cores = 2
    zs = 8
    xs = link_devs // (zs * cores)

    def shifted(block, move):
        pairs = [(src, move(src)) for src in range(link_devs)]
        return lax.ppermute(block, "link", pairs)

    def zmove(step):
        return lambda l: (l // (zs * cores)) * zs * cores + (((l // cores) % zs + step) % zs) * cores + l % cores

    def xmove(step):
        return lambda l: ((l // (zs * cores) + step) % xs) * zs * cores + l % (zs * cores)

    got = jnp.stack([part] + [shifted(part, zmove(s)) for s in range(1, zs)], 0)
    got = jnp.concatenate([got] + [shifted(got, xmove(s)) for s in range(1, xs)], 0)
    return jnp.concatenate([got, shifted(got, lambda l: l ^ 1)], 0)


def contract_rows(left_side, right_side):
    return lax.dot_general(
        left_side, right_side, (((0,), (0,)), ((), ())), preferred_element_type=jnp.float32
    )


def lower_inverse(lower):
    eye = jnp.eye(lower.shape[0], dtype=jnp.float32)
    return jax.scipy.linalg.solve_triangular(lower, eye, lower=True)


def solve_rows(block, inv_lower):
    return lax.dot_general(
        block, inv_lower, (((1,), (1,)), ((), ())), precision=HI,
        preferred_element_type=jnp.float32,
    )


def head_fix(solved, at_top, head):
    top = jnp.where(at_top, head, solved[: head.shape[0]])
    return jnp.concatenate([top, solved[head.shape[0]:]], 0)


def local(values, tiles, barrier, slack, order):
    link_devs = lax.axis_size("link")
    col_devs = lax.axis_size("col")
    link_idx = lax.axis_index("link")
    col_idx = lax.axis_index("col")
    link_count = slack.shape[0]
    rows_dev = link_count // link_devs
    cols_dev = link_count // col_devs
    per_dev, tpc, tile_len = values.shape
    ntiles = order.shape[0]
    lead = 2 * PANEL
    lead_tiles = lead // tile_len
    row_tiles = rows_dev // tile_len
    col_tiles = cols_dev // tile_len
    factor = link_count / (per_dev * link_devs * tpc * tile_len)
    scaled = (jnp.sqrt(barrier * factor)[:, None, None] * values.astype(jnp.float32)).astype(
        jnp.bfloat16
    )
    own_rows = scaled.reshape(per_dev * tpc, tile_len)
    own_ids = jnp.pad(tiles.astype(jnp.bfloat16), ((0, 0), (0, tile_len - tpc)))
    packed = jnp.concatenate([own_rows, own_ids], 0)
    groups = per_dev // SUB
    own_lead = densify(
        own_rows.reshape(groups, SUB * tpc, tile_len), tiles.reshape(groups, SUB * tpc),
        order[:lead_tiles],
    )
    copies = jnp.broadcast_to(own_lead[None], (link_devs,) + own_lead.shape)
    inc_lead = lax.all_to_all(copies, "link", 0, 0, tiled=True).reshape(-1, lead)
    everyone = lax.all_gather(packed, "link", axis=0)
    devs = everyone.shape[0]
    ids_all = everyone[:, per_dev * tpc:, :tpc].astype(jnp.int32)
    ids_all = ids_all.reshape(devs * groups, SUB * tpc)
    vals_all = everyone[:, : per_dev * tpc].reshape(devs * groups, SUB * tpc, tile_len)

    inc_rows = densify(
        vals_all, ids_all, lax.dynamic_slice_in_dim(order, link_idx * row_tiles, row_tiles)
    )
    inc_cols = densify(
        vals_all, ids_all, lax.dynamic_slice_in_dim(order, col_idx * col_tiles, col_tiles)
    )

    slack_ord = jnp.take(slack.reshape(ntiles, tile_len), order, axis=0).reshape(link_count)
    rows_g = link_idx * rows_dev + jnp.arange(rows_dev)
    cols_g = col_idx * cols_dev + jnp.arange(cols_dev)
    lead_g = jnp.arange(lead)

    def lead_cols(inc_x, x_g, start):
        base = contract_rows(inc_x, inc_lead)
        slack_x = lax.dynamic_slice_in_dim(slack_ord, start, x_g.shape[0])
        diag = jnp.where(x_g[:, None] == lead_g[None, :], slack_x[:, None], 0.0)
        return base + diag

    a_lead = lead_cols(inc_lead, lead_g, 0)
    f0, f1 = 0, PANEL
    l0 = jnp.linalg.cholesky(a_lead[f0:f1, f0:f1])
    inv0 = lower_inverse(l0)
    b0 = solve_rows(a_lead[f1:, f0:f1], inv0)
    head0 = jnp.concatenate([l0, b0], 0)
    rb0 = b0.astype(jnp.bfloat16)
    a11 = a_lead[f1:, f1:] - lax.dot_general(
        rb0, rb0, (((1,), (1,)), ((), ())), preferred_element_type=jnp.float32
    )
    l1 = jnp.linalg.cholesky(a11)
    inv1 = lower_inverse(l1)
    head1 = jnp.concatenate([jnp.zeros_like(l1), l1], 0)

    m_rows = lead_cols(inc_rows, rows_g, link_idx * rows_dev)
    m_cols = lead_cols(inc_cols, cols_g, col_idx * cols_dev)

    def panels(m_x, at_top):
        col0 = head_fix(solve_rows(m_x[:, f0:f1], inv0), at_top, head0)
        r0 = col0.astype(jnp.bfloat16)
        m1 = m_x[:, f1:] - lax.dot_general(
            r0, rb0, (((1,), (1,)), ((), ())), preferred_element_type=jnp.float32
        )
        col1 = head_fix(solve_rows(m1, inv1), at_top, head1)
        return col0, col1

    col0_r, col1_r = panels(m_rows, link_idx == 0)
    col0_c, col1_c = panels(m_cols, col_idx == 0)
    left_t = jnp.concatenate(
        [inc_rows, col0_r.astype(jnp.bfloat16).T, col1_r.astype(jnp.bfloat16).T], 0
    )
    right_t = jnp.concatenate(
        [inc_cols, -col0_c.astype(jnp.bfloat16).T, -col1_c.astype(jnp.bfloat16).T], 0
    )
    matrix = contract_rows(left_t, right_t)
    slack_rows = lax.dynamic_slice_in_dim(slack_ord, link_idx * rows_dev, rows_dev)
    matrix = matrix + jnp.where(
        rows_g[:, None] == cols_g[None, :], slack_rows[:, None], jnp.float32(0.0)
    )
    panel_block = jnp.concatenate([col0_r, col1_r], 1)
    padded = jnp.pad(panel_block, ((0, 0), (0, cols_dev - lead)))
    return jnp.where(
        cols_g[None, :] < lead,
        padded,
        jnp.where(rows_g[:, None] < lead, jnp.float32(0.0), matrix),
    )


def solution(mesh):
    in_specs = (P("link", None, None), P("link", None), P("link"), P(), P())
    out_specs = P("link", "col")
    return jax.shard_map(local, mesh=mesh, in_specs=in_specs, out_specs=out_specs, check_vma=False)
```

profile of v0, /device:TPU:1, one launch (start us, length us, event | category | flops | bytes accessed | tf_op | source)
XLA Modules:
  0.0 136.0 jit_solution(16664289943102642381)
XLA Ops:
  6.5 0.7 multiply_sqrt_fusion
  7.2 0.7 convert_element_type.82
  7.9 0.9 multiply_convert_fusion
  8.9 0.6 fusion.39
  9.5 0.8 eq.166
  10.3 0.8 fusion.55
  11.3 0.8 broadcast_in_dim.115
  12.2 13.0 %all-to-all-start = ((bf16[64,16,256]{2,1,0:T(8,128)(2,1)}), bf16[64,16,256]{2,1,0:T(8,128)(2,1)S(1)}, u32[]{:S(2)}, u32[]{:S(2)}) async-start(bf16[64,16,256]{2,1,0:T(8,128)(2,1)} %broadcast_in_dim.115), calls=%async_computation | async-start | bytes 1048576 | tf_op jit(solution)/shard_map/all_to_all | solution.py:95
  25.2 0.7 compare_select_fusion
  25.8 0.6 gather_fusion
  26.5 0.7 compare_and_fusion
  27.2 0.5 broadcast_compare_fusion.1
  27.8 0.7 dynamic_slice.19
  28.6 0.6 broadcast_compare_fusion
  29.3 14.5 %all-to-all-done = bf16[64,16,256]{2,1,0:T(8,128)(2,1)S(1)} async-done(((bf16[64,16,256]{2,1,0:T(8,128)(2,1)}), bf16[64,16,256]{2,1,0:T(8,128)(2,1)S(1)}, u32[]{:S(2)}, u32[]{:S(2)}) %all-to-all-start) | async-done | bytes 524320 | tf_op jit(solution)/shard_map/all_to_all | solution.py:95
  43.8 0.3 fusion.21
  44.3 11.7 %cholesky.44 = f32[128,128]{1,0:T(8,128)S(1)} custom-call(f32[128,128]{1,0:T(8,128)S(1)} %fusion.45), custom_call_target="Cholesky" | custom-call | tf_op jit(solution)/shard_map/jit(cholesky)/cholesky | solution.py:122
  56.1 0.6 compare_reduce_fusion.1
  56.7 0.7 select_bitcast_fusion.1
  57.4 9.8 %custom-call.6 = f32[1,128,128]{1,2,0:T(8,128)S(1)} custom-call(f32[1,128,128]{2,1,0:T(8,128)S(1)} %get-tuple-element.9), custom_call_target="InvertDiagBlocksLowerTriangular" | custom-call | tf_op jit(solution)/shard_map/jit(_solve_triangular)/triangular_solve | solution.py:53
  67.2 0.3 fusion.37
  67.5 0.3 fusion.40
  68.0 11.7 %cholesky.55 = f32[128,128]{1,0:T(8,128)S(1)} custom-call(f32[128,128]{1,0:T(8,128)S(1)} %fusion.43), custom_call_target="Cholesky" | custom-call | tf_op jit(solution)/shard_map/jit(cholesky)/cholesky | solution.py:130
  79.8 0.6 compare_reduce_fusion
  80.4 0.7 select_bitcast_fusion
  81.1 10.0 %custom-call.7 = f32[1,128,128]{1,2,0:T(8,128)S(1)} custom-call(f32[1,128,128]{2,1,0:T(8,128)S(1)} %get-tuple-element.6), custom_call_target="InvertDiagBlocksLowerTriangular" | custom-call | tf_op jit(solution)/shard_map/jit(_solve_triangular)/triangular_solve | solution.py:53
  91.1 0.3 fusion.35
  91.4 3.5 %all-gather.3.cloned.1.call-done = bf16[17408,128]{1,0:T(8,128)(2,1)} async-done(((bf16[272,128]{1,0:T(8,128)(2,1)}), bf16[17408,128]{1,0:T(8,128)(2,1)}) %all-gather.3.cloned.1.call-update) | async-done | bytes 4456464 | tf_op jit(solution)/shard_map/all_gather | solution.py:96
  94.8 1.0 slice_convert_fusion.2
  95.9 4.7 %slice.72 = bf16[64,256,128]{2,1,0:T(8,128)(2,1)} slice(bf16[64,272,128]{2,1,0:T(8,128)(2,1)} %bitcast.93), slice={[0:64], [0:256], [0:128]} | slice | bytes 8388608 | tf_op jit(solution)/shard_map/slice | solution.py:100
  100.6 0.2 reshape.159
  100.9 3.5 %fusion.20 = bf16[1024,256]{1,0:T(8,128)(2,1)S(1)} fusion(bf16[128,128,128]{2,1,0:T(8,128)(2,1)} %bitcast.90, bf16[16,128]{1,0:T(8,128)(2,1)S(1)} %broadcast_bitcast_fusion.1, bf16[128,2,128]{2,1,0:T(2,128)(2,1)S(1)} %compare_convert_fusion.1), kind=kOutput, calls=%fused_computation.26 | convolution fusion | flops 67633152 | bytes 4788224 | tf_op jit(solution)/shard_map/dot_general | solution.py:18
  104.4 0.4 convolution_add_fusion.1
  104.8 0.4 copy-done.2
  105.2 0.4 convolution_select_fusion.1
  105.8 0.3 compare_convert_fusion
  106.1 2.6 %convert_bitcast_fusion = bf16[1024,4096]{1,0:T(8,128)(2,1)S(1)} fusion(bf16[128,128,128]{2,1,0:T(8,128)(2,1)S(1)} %bitcast.91, bf16[256,128]{1,0:T(8,128)(2,1)S(1)} %broadcast_bitcast_fusion, bf16[128,32,128]{2,1,0:T(8,128)(2,1)S(1)} %compare_convert_fusion), kind=kOutput, calls=%fused_computation.9 | convolution fusion | flops 1082130432 | bytes 13697024 | tf_op jit(solution)/shard_map/dot_general | solution.py:18
  108.7 4.9 %convolution_add_fusion = f32[4096,256]{1,0:T(8,128)S(1)} fusion(bf16[1024,4096]{1,0:T(8,128)(2,1)S(1)} %convert_bitcast_fusion, bf16[1024,256]{1,0:T(8,128)(2,1)S(1)} %bitcast.97, f32[4096]{0:T(1024)S(1)} %dynamic-slice-done, s32[4096]{0:T(1024)S(1)} %iota_add_fusion), kind=kOutput, calls=%fused_computation.11 | convolution fusion | flops 2150629376 | bytes 13139968 | tf_op jit(solution)/shard_map/dot_general | solution.py:46
  113.6 1.8 %fusion.18 = bf16[4096,128]{1,0:T(8,128)(2,1)S(1)} fusion(f32[128,128]{1,0:T(8,128)S(1)} %fusion.37, f32[4096,256]{1,0:T(8,128)S(1)} %convolution_add_fusion), kind=kOutput, calls=%fused_computation.20 | convolution fusion | flops 805306368 | bytes 3211264 | tf_op jit(solution)/shard_map/dot_general | solution.py:57
  115.5 0.4 convolution_subtract_fusion
  116.0 0.2 negate_bitcast_fusion
  116.2 1.8 %fusion.56 = bf16[4096,128]{1,0:T(8,128)(2,1)S(1)} fusion(f32[4096,128]{1,0:T(8,128)S(1)} %convolution_subtract_fusion, f32[128,128]{1,0:T(8,128)S(1)} %fusion.35), kind=kOutput, calls=%fused_computation.115 | convolution fusion | flops 805306368 | bytes 3211264 | tf_op jit(solution)/shard_map/dot_general | solution.py:57
  118.1 0.4 convolution_select_fusion
  118.6 0.7 copy.39
  119.4 0.2 fusion.23
  119.6 1.4 %copy.42 = bf16[128,4096]{1,0:T(8,128)(2,1)} copy(bf16[128,4096]{0,1:T(8,128)(2,1)S(1)} %fusion.23) | data formatting | bytes 2097152 | tf_op jit(solution)/shard_map/neg | solution.py:152
  121.0 0.5 copy.41
  121.5 7.7 %fusion.13 = f32[256,4096]{1,0:T(8,128)} fusion(bf16[128,4096]{1,0:T(8,128)(2,1)} %copy.42, bf16[128,4096]{1,0:T(8,128)(2,1)S(1)} %copy.41, bf16[1024,4096]{1,0:T(8,128)(2,1)} %copy-done.7, f32[256,128]{1,0:T(8,128)S(1)} %convolution_select_fusion, f32[256,128]{1,0:T(8,128)S(1)} %convolution_select_fusion.1, f32[256]{0:T(256)} %copy-done.5, ...), kind=kOutput, calls=%fused_computation.13 | convolution fusion | flops 2727215104 | bytes 15620352 | tf_op jit(solution)/shard_map/dot_general | solution.py:46
  (49 shorter events, 1.6 us)
Async XLA Ops:
  6.5 19.3 %copy-start = (f32[16384]{0:T(1024)S(1)}, f32[16384]{0:T(1024)}, u32[]{:S(2)}) copy-start(f32[16384]{0:T(1024)} %param.11) | copy-start | bytes 196612
  6.5 88.3 %all-gather.3.cloned.1.call-start = ((), (), s32[]{:S(2)}) async-start(), calls=%async_computation.1 | async-start | bytes 4526080 | tf_op jit(solution)/shard_map/all_gather | solution.py:96
  12.2 31.7 %all-to-all-start = ((bf16[64,16,256]{2,1,0:T(8,128)(2,1)}), bf16[64,16,256]{2,1,0:T(8,128)(2,1)S(1)}, u32[]{:S(2)}, u32[]{:S(2)}) async-start(bf16[64,16,256]{2,1,0:T(8,128)(2,1)} %broadcast_in_dim.115), calls=%async_computation | async-start | bytes 1048576 | tf_op jit(solution)/shard_map/all_to_all | solution.py:95
  27.2 73.3 %copy-start.3 = (f32[16384]{0:T(1024)}, f32[16384]{0:T(1024)S(1)}, u32[]{:S(2)}) copy-start(f32[16384]{0:T(1024)S(1)} %fusion.73) | copy-start | bytes 196612
  28.6 75.8 %copy-start.5 = (f32[256]{0:T(256)}, f32[256]{0:T(256)S(1)}, u32[]{:S(2)}) copy-start(f32[256]{0:T(256)S(1)} %dynamic_slice.18) | copy-start | bytes 3076
  28.6 75.8 %copy-start.6 = (s32[256]{0:T(256)}, s32[256]{0:T(256)S(1)}, u32[]{:S(2)}) copy-start(s32[256]{0:T(256)S(1)} %iota_add_fusion.1) | copy-start | bytes 3076
  100.9 5.2 %copy-start.1 = (bf16[64,256,128]{2,1,0:T(8,128)(2,1)S(1)}, bf16[64,256,128]{2,1,0:T(8,128)(2,1)}, u32[]{:S(2)}) copy-start(bf16[64,256,128]{2,1,0:T(8,128)(2,1)} %slice.72) | copy-start | bytes 12582916
  104.4 0.8 copy-start.2
  106.1 2.6 %dynamic-slice-start = ((f32[16384]{0:T(1024)}, s32[]{:T(128)}), f32[4096]{0:T(1024)S(1)}, s32[]{:S(2)}) async-start(f32[16384]{0:T(1024)} %copy-done.3, s32[]{:T(128)} %select_n.103), calls=%async_computation.2 | async-start | bytes 33280 | tf_op jit(solution)/shard_map/dynamic_slice | solution.py:116
  108.7 4.9 %copy-start.7 = (bf16[1024,4096]{1,0:T(8,128)(2,1)}, bf16[1024,4096]{1,0:T(8,128)(2,1)S(1)}, u32[]{:S(2)}) copy-start(bf16[1024,4096]{1,0:T(8,128)(2,1)S(1)} %convert_bitcast_fusion) | copy-start | bytes 25165828
  119.6 1.9 %copy-start.4 = (bf16[128,256]{1,0:T(8,128)(2,1)S(1)}, bf16[128,256]{1,0:T(8,128)(2,1)}, u32[]{:S(2)}) copy-start(bf16[128,256]{1,0:T(8,128)(2,1)} %copy.39) | copy-start | bytes 196612
Sparse Core Ops, SparseCore 0:
  10.0 84.7 all-gather.2
where the time goes:
time: 136 us
  other arithmetic  53.5 us (39%)
  matrix products  25.4 us (19%)
  waiting for transfers between devices  18 us (13%)
  between operations  13.8 us (10%)
  starting transfers between devices  13 us (10%)
  local copies, waits for them, and re-layouts  12.3 us (9%)
    another operation x4, other arithmetic, lower_inverse(): return jax.scipy.linalg.solve_triangular(lower, eye, lower=True)  21.1 us
    all_to_all x1, waiting for transfers between devices, local(): lax.all_to_all(copies, 'link', 0, 0, tiled=True).reshape(-1, lead)  14.5 us
    dot_general x4, matrix products, contract_rows(): lax.dot_general(left_side, right_side, (((0,), (0,)), ((), ())), preferre...  13.2 us
    all_to_all x1, starting transfers between devices, local(): lax.all_to_all(copies, 'link', 0, 0, tiled=True).reshape(-1, lead)  13 us
    another operation x3, other arithmetic, local(): l0 = jnp.linalg.cholesky(a_lead[f0:f1, f0:f1])  12.4 us
    another operation x3, other arithmetic, local(): l1 = jnp.linalg.cholesky(a11)  12.4 us
    dot_general x3, matrix products, densify(): lax.dot_general(spread, vals, (((2,), (1,)), ((0,), (0,))), preferred_ele...  6.2 us
    slice x1, local copies, waits for them, and re-layouts, local(): everyone[:, :per_dev * tpc].reshape(devs * groups, SUB * tpc, tile_len)  4.7 us
  transfers between devices with their start and end apart: 2, of which 2 were waited for; matrix products, arithmetic and copies ran while one was open for 40% of the time, Pallas kernels for 0%

commit v1 on v0

--- a/solution.py
+++ b/solution.py
@@ -84,20 +84,21 @@
         jnp.bfloat16
     )
     own_rows = scaled.reshape(per_dev * tpc, tile_len)
-    own_ids = jnp.pad(tiles.astype(jnp.bfloat16), ((0, 0), (0, tile_len - tpc)))
-    packed = jnp.concatenate([own_rows, own_ids], 0)
     groups = per_dev // SUB
     own_lead = densify(
         own_rows.reshape(groups, SUB * tpc, tile_len), tiles.reshape(groups, SUB * tpc),
         order[:lead_tiles],
     )
-    copies = jnp.broadcast_to(own_lead[None], (link_devs,) + own_lead.shape)
-    inc_lead = lax.all_to_all(copies, "link", 0, 0, tiled=True).reshape(-1, lead)
-    everyone = lax.all_gather(packed, "link", axis=0)
+    own_ids = jnp.pad(tiles.astype(jnp.bfloat16), ((0, 0), (0, tile_len - tpc)))
+    small = jnp.concatenate([own_lead, own_ids], 1)
+    copies = jnp.broadcast_to(small[None], (link_devs,) + small.shape)
+    small_all = lax.all_to_all(copies, "link", 0, 0, tiled=True).reshape(-1, lead + tile_len)
+    inc_lead = small_all[:, :lead]
+    everyone = lax.all_gather(own_rows, "link", axis=0)
     devs = everyone.shape[0]
-    ids_all = everyone[:, per_dev * tpc:, :tpc].astype(jnp.int32)
+    ids_all = small_all[:, lead : lead + tpc].astype(jnp.int32)
     ids_all = ids_all.reshape(devs * groups, SUB * tpc)
-    vals_all = everyone[:, : per_dev * tpc].reshape(devs * groups, SUB * tpc, tile_len)
+    vals_all = everyone.reshape(devs * groups, SUB * tpc, tile_len)
 
     inc_rows = densify(
         vals_all, ids_all, lax.dynamic_slice_in_dim(order, link_idx * row_tiles, row_tiles)

time: 136 us -> 134 us (0.985)
  local copies, waits for them, and re-layouts: 12.3 us -> 6.71 us
  waiting for transfers between devices: 18 us -> 20.8 us
    all_to_all x1, waiting for transfers between devices: 14.5 us -> 20.8 us  [local(): lax.all_to_all(copies, 'link', 0, 0, tiled=True)]
    slice x1 -> x0, local copies, waits for them, and re-layouts: 4.7 us -> none  [local(): everyone[:, :per_dev * tpc].reshape(devs * groups, SUB * tpc, tile_len)]
    all_gather x1, waiting for transfers between devices: 3.48 us -> 0.02 us  [local(): everyone = lax.all_gather(own_rows, 'link', axis=0)]
  transfers between devices with their start and end apart: 2 -> 2, of which waited for: 2 -> 1; matrix products, arithmetic and copies ran while one was open for 40% -> 42% of each run, Pallas kernels for 0% -> 0%
where the time goes in v1:
time: 134 us
  other arithmetic  54.6 us (41%)
  matrix products  24.9 us (19%)
  waiting for transfers between devices  20.8 us (16%)
  between operations  13.8 us (10%)
  starting transfers between devices  13 us (10%)
  local copies, waits for them, and re-layouts  6.71 us (5%)
    another operation x4, other arithmetic, lower_inverse(): return jax.scipy.linalg.solve_triangular(lower, eye, lower=True)  21.1 us
    all_to_all x1, waiting for transfers between devices, local(): lax.all_to_all(copies, 'link', 0, 0, tiled=True)  20.8 us
    all_to_all x1, starting transfers between devices, local(): lax.all_to_all(copies, 'link', 0, 0, tiled=True)  13 us
    another operation x3, other arithmetic, local(): l0 = jnp.linalg.cholesky(a_lead[f0:f1, f0:f1])  12.4 us
    another operation x3, other arithmetic, local(): l1 = jnp.linalg.cholesky(a11)  12.4 us
    dot_general x4, matrix products, contract_rows(): lax.dot_general(left_side, right_side, (((0,), (0,)), ((), ())), preferre...  11.9 us
    dot_general x3, matrix products, densify(): lax.dot_general(spread, vals, (((2,), (1,)), ((0,), (0,))), preferred_ele...  7.03 us
    dot_general x5, matrix products, solve_rows(): lax.dot_general(block, inv_lower, (((1,), (1,)), ((), ())), precision=HI,...  4.66 us
  transfers between devices with their start and end apart: 2, of which 1 were waited for; matrix products, arithmetic and copies ran while one was open for 42% of the time, Pallas kernels for 0%

profile of v1, /device:TPU:1, one launch (start us, length us, event | category | flops | bytes accessed | tf_op | source)
XLA Modules:
  0.0 133.8 jit_solution(1800911465274284332)
XLA Ops:
  6.5 0.7 multiply_sqrt_fusion
  7.2 1.6 %multiply_convert_fusion = bf16[16,16,128]{2,1,0:T(8,128)(2,1)} fusion(bf16[16,16,128]{2,1,0:T(8,128)(2,1)} %param.8, f32[16]{0:T(128)S(1)} %multiply_sqrt_fusion), kind=kLoop, calls=%fused_computation.60 | loop fusion | flops 98304 | bytes 131136 | tf_op jit(solution)/shard_map/convert_element_type | solution.py:83
  8.8 0.8 eq.166
  9.6 0.7 convert_element_type.81
  10.3 0.8 fusion.57
  11.2 1.0 fusion.21
  12.2 1.0 broadcast_in_dim.75
  13.1 13.0 %all-to-all-start = ((bf16[64,16,384]{2,1,0:T(8,128)(2,1)}), bf16[64,16,384]{2,1,0:T(8,128)(2,1)S(1)}, u32[]{:S(2)}, u32[]{:S(2)}) async-start(bf16[64,16,384]{2,1,0:T(8,128)(2,1)} %broadcast_in_dim.75), calls=%async_computation | async-start | bytes 1572864 | tf_op jit(solution)/shard_map/all_to_all | solution.py:95
  26.1 0.7 dynamic_slice.19
  26.8 0.7 compare_select_fusion
  27.5 0.6 gather_fusion
  28.2 0.7 compare_and_fusion
  29.0 0.5 broadcast_compare_fusion.1
  29.6 0.6 broadcast_compare_fusion
  30.3 20.8 %all-to-all-done = bf16[64,16,384]{2,1,0:T(8,128)(2,1)S(1)} async-done(((bf16[64,16,384]{2,1,0:T(8,128)(2,1)}), bf16[64,16,384]{2,1,0:T(8,128)(2,1)S(1)}, u32[]{:S(2)}, u32[]{:S(2)}) %all-to-all-start) | async-done | bytes 786464 | tf_op jit(solution)/shard_map/all_to_all | solution.py:95
  51.1 0.3 convolution_add_fusion.2
  51.6 11.7 %cholesky.44 = f32[128,128]{1,0:T(8,128)S(1)} custom-call(f32[128,128]{1,0:T(8,128)S(1)} %fusion.45), custom_call_target="Cholesky" | custom-call | tf_op jit(solution)/shard_map/jit(cholesky)/cholesky | solution.py:123
  63.3 0.6 compare_reduce_fusion.1
  63.9 0.7 select_bitcast_fusion.1
  64.6 9.8 %custom-call.6 = f32[1,128,128]{1,2,0:T(8,128)S(1)} custom-call(f32[1,128,128]{2,1,0:T(8,128)S(1)} %get-tuple-element.9), custom_call_target="InvertDiagBlocksLowerTriangular" | custom-call | tf_op jit(solution)/shard_map/jit(_solve_triangular)/triangular_solve | solution.py:53
  74.4 0.3 fusion.38
  74.7 0.3 fusion.40
  75.0 0.1 convolution_subtract_fusion.2
  75.3 11.7 %cholesky.55 = f32[128,128]{1,0:T(8,128)S(1)} custom-call(f32[128,128]{1,0:T(8,128)S(1)} %fusion.43), custom_call_target="Cholesky" | custom-call | tf_op jit(solution)/shard_map/jit(cholesky)/cholesky | solution.py:131
  87.0 0.6 compare_reduce_fusion
  87.7 0.7 select_bitcast_fusion
  88.3 10.0 %custom-call.7 = f32[1,128,128]{1,2,0:T(8,128)S(1)} custom-call(f32[1,128,128]{2,1,0:T(8,128)S(1)} %get-tuple-element.6), custom_call_target="InvertDiagBlocksLowerTriangular" | custom-call | tf_op jit(solution)/shard_map/jit(_solve_triangular)/triangular_solve | solution.py:53
  98.4 0.2 reshape.159
  98.6 0.3 fusion.36
  98.8 0.1 compare_convert_fusion.1
  99.0 0.3 compare_convert_fusion
  99.3 3.5 %fusion.20 = bf16[1024,256]{1,0:T(8,128)(2,1)S(1)} fusion(bf16[128,128,128]{2,1,0:T(8,128)(2,1)} %bitcast.81, bf16[16,128]{1,0:T(8,128)(2,1)S(1)} %broadcast_bitcast_fusion.1, bf16[128,2,128]{2,1,0:T(2,128)(2,1)S(1)} %compare_convert_fusion.1), kind=kOutput, calls=%fused_computation.26 | convolution fusion | flops 67633152 | bytes 4788224 | tf_op jit(solution)/shard_map/dot_general | solution.py:18
  102.9 0.4 convolution_add_fusion.1
  103.3 0.4 convolution_select_fusion.1
  103.6 0.2 convolution_subtract_fusion.1
  103.8 0.6 convert_bitcast_fusion.2
  104.5 2.5 %convert_bitcast_fusion = bf16[1024,4096]{1,0:T(8,128)(2,1)S(1)} fusion(bf16[128,128,128]{2,1,0:T(8,128)(2,1)S(1)} %bitcast.82, bf16[256,128]{1,0:T(8,128)(2,1)S(1)} %broadcast_bitcast_fusion, bf16[128,32,128]{2,1,0:T(8,128)(2,1)S(1)} %compare_convert_fusion), kind=kOutput, calls=%fused_computation.9 | convolution fusion | flops 1082130432 | bytes 13697024 | tf_op jit(solution)/shard_map/dot_general | solution.py:18
  107.0 3.5 %convolution_add_fusion = f32[4096,256]{1,0:T(8,128)S(1)} fusion(bf16[1024,4096]{1,0:T(8,128)(2,1)S(1)} %convert_bitcast_fusion, f32[4096]{0:T(1024)S(1)} %dynamic-slice-done, s32[4096]{0:T(1024)S(1)} %iota_add_fusion, bf16[1024,384]{1,0:T(8,128)(2,1)S(1)} %bitcast.86), kind=kOutput, calls=%fused_computation.11 | convolution fusion | flops 2150629376 | bytes 13139968 | tf_op jit(solution)/shard_map/dot_general | solution.py:46
  110.6 1.8 %fusion.18 = bf16[4096,128]{1,0:T(8,128)(2,1)S(1)} fusion(f32[128,128]{1,0:T(8,128)S(1)} %fusion.38, f32[4096,256]{1,0:T(8,128)S(1)} %convolution_add_fusion), kind=kOutput, calls=%fused_computation.20 | convolution fusion | flops 805306368 | bytes 3211264 | tf_op jit(solution)/shard_map/dot_general | solution.py:57
  112.5 0.4 convolution_subtract_fusion
  113.0 0.2 negate_bitcast_fusion
  113.2 1.8 %fusion.58 = bf16[4096,128]{1,0:T(8,128)(2,1)S(1)} fusion(f32[4096,128]{1,0:T(8,128)S(1)} %convolution_subtract_fusion, f32[128,128]{1,0:T(8,128)S(1)} %fusion.36), kind=kOutput, calls=%fused_computation.117 | convolution fusion | flops 805306368 | bytes 3211264 | tf_op jit(solution)/shard_map/dot_general | solution.py:57
  115.1 0.6 fusion.33
  115.7 0.4 convolution_select_fusion
  116.4 1.0 fusion.22
  117.4 1.4 %copy.39 = bf16[128,4096]{1,0:T(8,128)(2,1)} copy(bf16[128,4096]{0,1:T(8,128)(2,1)S(1)} %fusion.22) | data formatting | bytes 2097152 | tf_op jit(solution)/shard_map/neg | solution.py:153
  118.8 0.5 copy.38
  119.3 7.7 %fusion.13 = f32[256,4096]{1,0:T(8,128)} fusion(bf16[128,4096]{1,0:T(8,128)(2,1)} %copy.39, bf16[128,4096]{1,0:T(8,128)(2,1)S(1)} %copy.38, bf16[1024,4096]{1,0:T(8,128)(2,1)} %copy-done.7, f32[256,128]{1,0:T(8,128)S(1)} %convolution_select_fusion, f32[256,128]{1,0:T(8,128)S(1)} %convolution_select_fusion.1, f32[256]{0:T(256)} %copy-done.5, ...), kind=kOutput, calls=%fused_computation.13 | convolution fusion | flops 2727215104 | bytes 15620352 | tf_op jit(solution)/shard_map/dot_general | solution.py:46
  (48 shorter events, 1.2 us)
Async XLA Ops:
  6.5 21.0 %copy-start = (f32[16384]{0:T(1024)S(1)}, f32[16384]{0:T(1024)}, u32[]{:S(2)}) copy-start(f32[16384]{0:T(1024)} %param.11) | copy-start | bytes 196612
  6.5 92.8 %all-gather.2.cloned.1.call-start = ((), (), s32[]{:S(2)}) async-start(), calls=%async_computation.1 | async-start | bytes 4259840 | tf_op jit(solution)/shard_map/all_gather | solution.py:97
  13.1 38.0 %all-to-all-start = ((bf16[64,16,384]{2,1,0:T(8,128)(2,1)}), bf16[64,16,384]{2,1,0:T(8,128)(2,1)S(1)}, u32[]{:S(2)}, u32[]{:S(2)}) async-start(bf16[64,16,384]{2,1,0:T(8,128)(2,1)} %broadcast_in_dim.75), calls=%async_computation | async-start | bytes 1572864 | tf_op jit(solution)/shard_map/all_to_all | solution.py:95
  28.9 73.9 %copy-start.4 = (f32[16384]{0:T(1024)}, f32[16384]{0:T(1024)S(1)}, u32[]{:S(2)}) copy-start(f32[16384]{0:T(1024)S(1)} %fusion.71) | copy-start | bytes 196612
  29.0 73.8 %copy-start.5 = (f32[256]{0:T(256)}, f32[256]{0:T(256)S(1)}, u32[]{:S(2)}) copy-start(f32[256]{0:T(256)S(1)} %dynamic_slice.18) | copy-start | bytes 3076
  29.6 73.3 %copy-start.6 = (s32[256]{0:T(256)}, s32[256]{0:T(256)S(1)}, u32[]{:S(2)}) copy-start(s32[256]{0:T(256)S(1)} %iota_add_fusion.1) | copy-start | bytes 3076
  99.3 5.1 %copy-start.1 = (bf16[64,256,128]{2,1,0:T(8,128)(2,1)S(1)}, bf16[64,256,128]{2,1,0:T(8,128)(2,1)}, u32[]{:S(2)}) copy-start(bf16[64,256,128]{2,1,0:T(8,128)(2,1)} %all-gather.2.cloned.1.call-done) | copy-start | bytes 12582916
  102.9 4.1 %copy-start.2 = (bf16[1024,256]{1,0:T(8,128)(2,1)}, bf16[1024,256]{1,0:T(8,128)(2,1)S(1)}, u32[]{:S(2)}) copy-start(bf16[1024,256]{1,0:T(8,128)(2,1)S(1)} %fusion.20) | copy-start | bytes 1572868
  104.5 2.6 %dynamic-slice-start = ((f32[16384]{0:T(1024)}, s32[]{:T(128)}), f32[4096]{0:T(1024)S(1)}, s32[]{:S(2)}) async-start(f32[16384]{0:T(1024)} %copy-done.4, s32[]{:T(128)} %select_n.103), calls=%async_computation.2 | async-start | bytes 33280 | tf_op jit(solution)/shard_map/dynamic_slice | solution.py:117
  107.0 3.6 %copy-start.7 = (bf16[1024,4096]{1,0:T(8,128)(2,1)}, bf16[1024,4096]{1,0:T(8,128)(2,1)S(1)}, u32[]{:S(2)}) copy-start(bf16[1024,4096]{1,0:T(8,128)(2,1)S(1)} %convert_bitcast_fusion) | copy-start | bytes 25165828
  113.0 3.3 %copy-start.3 = (bf16[128,256]{0,1:T(8,128)(2,1)S(1)}, bf16[128,256]{0,1:T(8,128)(2,1)}, u32[]{:S(2)}) copy-start(bf16[128,256]{0,1:T(8,128)(2,1)} %convert_bitcast_fusion.2) | copy-start | bytes 196612
Sparse Core Ops, SparseCore 0:
  10.1 84.3 all-gather.1

commit v2 on v1

--- a/solution.py
+++ b/solution.py
@@ -2,10 +2,61 @@
 import jax.numpy as jnp
 from jax import lax
 from jax.sharding import PartitionSpec as P
+from jax.experimental import pallas as pl
+from jax.experimental.pallas import tpu as pltpu
 
 PANEL = 128
 SUB = 8
 HI = lax.Precision.HIGHEST
+BLK = 8
+
+
+def _chol_inv_kernel(a_ref, lt_ref, inv_ref, work, binv):
+    n = a_ref.shape[0]
+    work[...] = a_ref[...]
+    rr = lax.broadcasted_iota(jnp.int32, (n, n), 0)
+    cc = lax.broadcasted_iota(jnp.int32, (n, n), 1)
+    binv[...] = jnp.where(rr == cc, 1.0, 0.0).astype(jnp.float32)
+    lane = lax.broadcasted_iota(jnp.int32, (BLK, n), 1)
+    sub = lax.broadcasted_iota(jnp.int32, (BLK, n), 0)
+    subc = lax.broadcasted_iota(jnp.int32, (BLK, 1), 0)
+
+    def block(b, carry):
+        base = pl.multiple_of(b * BLK, BLK)
+        slab = work[pl.ds(base, BLK), :]
+        bslab = binv[pl.ds(base, BLK), :]
+        out = jnp.zeros((BLK, n), jnp.float32)
+        xout = jnp.zeros((BLK, n), jnp.float32)
+        for i in range(BLK):
+            col = base + i
+            rowi = jnp.sum(jnp.where(sub == i, slab, 0.0), axis=0, keepdims=True)
+            d = jnp.sum(jnp.where(lane[0:1] == col, rowi, 0.0), axis=1, keepdims=True)
+            s = 1.0 / jnp.sqrt(d)
+            lrow = jnp.where(lane[0:1] >= col, rowi * s, 0.0)
+            out = jnp.where(sub == i, lrow, out)
+            colv = jnp.sum(jnp.where(lane == col, slab, 0.0), axis=1, keepdims=True) * s
+            slab = slab - colv * lrow
+            xi = jnp.sum(jnp.where(sub == i, bslab, 0.0), axis=0, keepdims=True) * s
+            xout = jnp.where(sub == i, xi, xout)
+            bslab = bslab - jnp.where(subc > i, colv, 0.0) * xi
+        lt_ref[pl.ds(base, BLK), :] = out
+        inv_ref[pl.ds(base, BLK), :] = xout
+        out_t = out.T
+        work[...] = work[...] - jnp.dot(out_t, out, precision=HI, preferred_element_type=jnp.float32)
+        binv[...] = binv[...] - jnp.dot(out_t, xout, precision=HI, preferred_element_type=jnp.float32)
+        return carry
+
+    lax.fori_loop(0, n // BLK, block, 0)
+
+
+def chol_inv(a):
+    n = a.shape[0]
+    lt, inv = pl.pallas_call(
+        _chol_inv_kernel,
+        out_shape=(jax.ShapeDtypeStruct((n, n), jnp.float32), jax.ShapeDtypeStruct((n, n), jnp.float32)),
+        scratch_shapes=[pltpu.VMEM((n, n), jnp.float32), pltpu.VMEM((n, n), jnp.float32)],
+    )(a)
+    return lt.T, inv
 
 
 def densify(vals, ids, targets):
@@ -120,16 +171,14 @@
 
     a_lead = lead_cols(inc_lead, lead_g, 0)
     f0, f1 = 0, PANEL
-    l0 = jnp.linalg.cholesky(a_lead[f0:f1, f0:f1])
-    inv0 = lower_inverse(l0)
+    l0, inv0 = chol_inv(a_lead[f0:f1, f0:f1])
     b0 = solve_rows(a_lead[f1:, f0:f1], inv0)
     head0 = jnp.concatenate([l0, b0], 0)
     rb0 = b0.astype(jnp.bfloat16)
     a11 = a_lead[f1:, f1:] - lax.dot_general(
         rb0, rb0, (((1,), (1,)), ((), ())), preferred_element_type=jnp.float32
     )
-    l1 = jnp.linalg.cholesky(a11)
-    inv1 = lower_inverse(l1)
+    l1, inv1 = chol_inv(a11)
     head1 = jnp.concatenate([jnp.zeros_like(l1), l1], 0)
 
     m_rows = lead_cols(inc_rows, rows_g, link_idx * rows_dev)

time: 134 us -> 141 us (1.052)
  other arithmetic: 54.6 us -> 8.16 us
  Pallas kernels: 0 us -> 37.9 us
  local copies, waits for them, and re-layouts: 6.71 us -> 14.6 us
  matrix products: 24.9 us -> 28.5 us
  waiting for transfers between devices: 20.8 us -> 23.8 us
    another operation x12 -> x2, other arithmetic: 46.5 us -> 0.87 us  [the longest x4 21.1 us: lower_inverse(): return jax.scipy.linalg.solve_triangular(lower, eye, lower=True)]
    pallas_call x0 -> x2, Pallas kernels: none -> 37.9 us  [chol_inv(): pl.pallas_call(_chol_inv_kernel, out_shape=(jax.ShapeDtypeStruct((n, n),...]
    select_n x0 -> x1, local copies, waits for them, and re-layouts: none -> 5.59 us  [local(): jnp.where(cols_g[None, :] < lead, padded, jnp.where(rows_g[:, None] < lea...]
    all_gather x1, waiting for transfers between devices: 0.02 us -> 3.04 us  [local(): everyone = lax.all_gather(own_rows, 'link', axis=0)]
    dot_general x2, matrix products: 0.61 us -> 2.22 us  [panels(): lax.dot_general(r0, rb0, (((1,), (1,)), ((), ())), preferred_element_type...]
  transfers between devices with their start and end apart: 2 -> 2, of which waited for: 1 -> 2; matrix products, arithmetic and copies ran while one was open for 42% -> 9% of each run, Pallas kernels for 0% -> 27%
where the time goes in v2:
time: 141 us; the launch traced here: 140 us
  Pallas kernels  37.9 us (27%)
  matrix products  28.5 us (20%)
  waiting for transfers between devices  23.8 us (17%)
  local copies, waits for them, and re-layouts  14.6 us (10%)
  between operations  13.8 us (10%)
  starting transfers between devices  13 us (9%)
  other arithmetic  8.16 us (6%)
    pallas_call x2, Pallas kernels, chol_inv(): pl.pallas_call(_chol_inv_kernel, out_shape=(jax.ShapeDtypeStruct((n, n),...  37.9 us
    all_to_all x1, waiting for transfers between devices, local(): lax.all_to_all(copies, 'link', 0, 0, tiled=True)  20.8 us
    dot_general x4, matrix products, contract_rows(): lax.dot_general(left_side, right_side, (((0,), (0,)), ((), ())), preferre...  13.1 us
    all_to_all x1, starting transfers between devices, local(): lax.all_to_all(copies, 'link', 0, 0, tiled=True)  13 us
    dot_general x3, matrix products, densify(): lax.dot_general(spread, vals, (((2,), (1,)), ((0,), (0,))), preferred_ele...  7.09 us
    select_n x1, local copies, waits for them, and re-layouts, local(): jnp.where(cols_g[None, :] < lead, padded, jnp.where(rows_g[:, None] < lea...  5.59 us
    dot_general x5, matrix products, solve_rows(): lax.dot_general(block, inv_lower, (((1,), (1,)), ((), ())), precision=HI,...  5.26 us
    all_gather x1, waiting for transfers between devices, local(): everyone = lax.all_gather(own_rows, 'link', axis=0)  3.04 us
  transfers between devices with their start and end apart: 2, of which 2 were waited for; matrix products, arithmetic and copies ran while one was open for 9% of the time, Pallas kernels for 27%

profile of v2, /device:TPU:1, one launch (start us, length us, event | category | flops | bytes accessed | tf_op | source)
XLA Modules:
  0.0 139.8 jit_solution(9255582168116856904)
XLA Ops:
  6.5 0.7 multiply_sqrt_fusion
  7.2 1.6 %multiply_convert_fusion = bf16[16,16,128]{2,1,0:T(8,128)(2,1)} fusion(bf16[16,16,128]{2,1,0:T(8,128)(2,1)} %param.5, f32[16]{0:T(128)S(1)} %multiply_sqrt_fusion), kind=kLoop, calls=%fused_computation.59 | loop fusion | flops 98304 | bytes 131136 | tf_op jit(solution)/shard_map/convert_element_type | solution.py:134
  8.8 0.8 eq.160
  9.6 0.7 convert_element_type.75
  10.3 0.8 fusion.48
  11.2 1.0 fusion.21
  12.2 1.0 broadcast_in_dim.74
  13.1 13.0 %all-to-all-start = ((bf16[64,16,384]{2,1,0:T(8,128)(2,1)}), bf16[64,16,384]{2,1,0:T(8,128)(2,1)S(1)}, u32[]{:S(2)}, u32[]{:S(2)}) async-start(bf16[64,16,384]{2,1,0:T(8,128)(2,1)} %broadcast_in_dim.74), calls=%async_computation | async-start | bytes 1572864 | tf_op jit(solution)/shard_map/all_to_all | solution.py:146
  26.1 0.7 dynamic_slice.19
  26.9 0.7 compare_select_fusion
  27.5 0.6 gather_fusion
  28.2 0.7 compare_and_fusion
  29.0 0.6 broadcast_compare_fusion.1
  29.6 0.6 broadcast_compare_fusion
  30.3 20.8 %all-to-all-done = bf16[64,16,384]{2,1,0:T(8,128)(2,1)S(1)} async-done(((bf16[64,16,384]{2,1,0:T(8,128)(2,1)}), bf16[64,16,384]{2,1,0:T(8,128)(2,1)S(1)}, u32[]{:S(2)}, u32[]{:S(2)}) %all-to-all-start) | async-done | bytes 786464 | tf_op jit(solution)/shard_map/all_to_all | solution.py:146
  51.1 0.3 convolution_add_fusion.2
  51.4 0.6 slice.62.a_ref
  52.1 19.0 %shard_map.55 = (f32[128,128]{1,0:T(8,128)}, f32[128,128]{1,0:T(8,128)}) custom-call(f32[128,128]{1,0:T(8,128)} %slice.62.a_ref), custom_call_target="tpu_custom_call" | custom-call | tf_op jit(solution)/shard_map/pallas_call | solution.py:54
  71.0 1.1 fusion.35
  72.2 0.8 convolution_subtract_fusion.2.a_ref
  73.0 19.0 %shard_map.56 = (f32[128,128]{1,0:T(8,128)}, f32[128,128]{1,0:T(8,128)}) custom-call(f32[128,128]{1,0:T(8,128)} %convolution_subtract_fusion.2.a_ref), custom_call_target="tpu_custom_call" | custom-call | tf_op jit(solution)/shard_map/pallas_call | solution.py:54
  92.1 0.2 reshape.151
  92.3 0.1 compare_convert_fusion.1
  92.4 0.3 compare_convert_fusion
  92.7 3.0 %all-gather.2.cloned.1.call-done = bf16[64,256,128]{2,1,0:T(8,128)(2,1)} async-done(((bf16[1,256,128]{2,1,0:T(8,128)(2,1)}), bf16[64,256,128]{2,1,0:T(8,128)(2,1)}) %all-gather.2.cloned.1.call-update) | async-done | bytes 4194320 | tf_op jit(solution)/shard_map/all_gather | solution.py:148
  95.7 4.9 %convert_bitcast_fusion = bf16[1024,4096]{1,0:T(8,128)(2,1)S(1)} fusion(bf16[128,128,128]{2,1,0:T(8,128)(2,1)} %bitcast.65, bf16[256,128]{1,0:T(8,128)(2,1)S(1)} %broadcast_bitcast_fusion, bf16[128,32,128]{2,1,0:T(8,128)(2,1)S(1)} %compare_convert_fusion), kind=kOutput, calls=%fused_computation.9 | convolution fusion | flops 1082130432 | bytes 13697024 | tf_op jit(solution)/shard_map/dot_general | solution.py:69
  100.7 3.5 %convolution_add_fusion = f32[4096,256]{1,0:T(8,128)S(1)} fusion(bf16[1024,4096]{1,0:T(8,128)(2,1)S(1)} %convert_bitcast_fusion, f32[4096]{0:T(1024)S(1)} %dynamic_slice.20, s32[4096]{0:T(1024)S(1)} %iota_add_fusion, bf16[1024,384]{1,0:T(8,128)(2,1)S(1)} %bitcast.69), kind=kOutput, calls=%fused_computation.11 | convolution fusion | flops 2150629376 | bytes 13139968 | tf_op jit(solution)/shard_map/dot_general | solution.py:97
  104.3 1.8 %fusion.18 = bf16[4096,128]{1,0:T(8,128)(2,1)S(1)} fusion(f32[128,128]{1,0:T(8,128)S(1)} %copy-done.4, f32[4096,256]{1,0:T(8,128)S(1)} %convolution_add_fusion), kind=kOutput, calls=%fused_computation.20 | convolution fusion | flops 805306368 | bytes 3211264 | tf_op jit(solution)/shard_map/dot_general | solution.py:108
  106.1 0.2 copy-done.3
  106.5 0.1 copy.26
  106.6 2.0 %convolution_subtract_fusion = f32[4096,128]{1,0:T(8,128)S(1)} fusion(f32[4096,256]{1,0:T(8,128)} %copy-done.3, bf16[3840,128]{1,0:T(8,128)(2,1)S(1)} %slice.93, bf16[256,128]{1,0:T(8,128)(2,1)S(1)} %copy.26, f32[128,128]{1,0:T(8,128)S(1)} %fusion.35), kind=kOutput, calls=%fused_computation.14 | convolution fusion | flops 136855552 | bytes 5308416 | tf_op jit(solution)/shard_map/dot_general | solution.py:190
  108.7 0.2 negate_bitcast_fusion
  108.9 1.8 %fusion.49 = bf16[4096,128]{1,0:T(8,128)(2,1)S(1)} fusion(f32[4096,128]{1,0:T(8,128)S(1)} %convolution_subtract_fusion, f32[128,128]{1,0:T(8,128)S(1)} %copy-done.7), kind=kOutput, calls=%fused_computation.96 | convolution fusion | flops 805306368 | bytes 3211264 | tf_op jit(solution)/shard_map/dot_general | solution.py:108
  110.7 0.7 slice.72
  111.4 1.2 fusion.20
  112.6 0.3 convolution_add_fusion.1
  113.0 0.3 convolution_select_fusion.1
  113.3 0.2 convolution_subtract_fusion.1
  113.5 0.3 convolution_select_fusion
  113.8 0.7 convert_bitcast_fusion.1
  114.5 0.5 copy.29
  115.0 0.9 copy.35
  115.9 0.9 fusion.33
  116.8 0.1 copy.28
  116.9 0.2 fusion.22
  117.1 1.3 copy.30
  118.5 8.9 %fusion.13 = f32[256,4096]{0,1:T(8,128)} fusion(bf16[128,4096]{1,0:T(8,128)(2,1)} %copy.30, bf16[128,4096]{1,0:T(8,128)(2,1)S(1)} %copy.29, bf16[1024,4096]{1,0:T(8,128)(2,1)} %copy-done.11, f32[256,128]{0,1:T(8,128)S(1)} %convolution_select_fusion, f32[256,128]{0,1:T(8,128)S(1)} %convolution_select_fusion.1, f32[256]{0:T(256)} %copy-done.9, ...), kind=kOutput, calls=%fused_computation.13 | convolution fusion | flops 2727215104 | bytes 15620352 | tf_op jit(solution)/shard_map/dot_general | solution.py:97
  127.3 5.6 %copy.32 = f32[256,4096]{1,0:T(8,128)} copy(f32[256,4096]{0,1:T(8,128)} %fusion.13) | data formatting | bytes 8388608 | tf_op jit(solution)/shard_map/jit(_where)/select_n | solution.py:211
  (47 shorter events, 0.8 us)
Async XLA Ops:
  6.5 21.0 %copy-start = (f32[16384]{0:T(1024)S(1)}, f32[16384]{0:T(1024)}, u32[]{:S(2)}) copy-start(f32[16384]{0:T(1024)} %param.8) | copy-start | bytes 196612
  6.5 89.2 %all-gather.2.cloned.1.call-start = ((), (), s32[]{:S(2)}) async-start(), calls=%async_computation.1 | async-start | bytes 4259840 | tf_op jit(solution)/shard_map/all_gather | solution.py:148
  13.1 38.0 %all-to-all-start = ((bf16[64,16,384]{2,1,0:T(8,128)(2,1)}), bf16[64,16,384]{2,1,0:T(8,128)(2,1)S(1)}, u32[]{:S(2)}, u32[]{:S(2)}) async-start(bf16[64,16,384]{2,1,0:T(8,128)(2,1)} %broadcast_in_dim.74), calls=%async_computation | async-start | bytes 1572864 | tf_op jit(solution)/shard_map/all_to_all | solution.py:146
  29.0 83.6 %copy-start.9 = (f32[256]{0:T(256)}, f32[256]{0:T(256)S(1)}, u32[]{:S(2)}) copy-start(f32[256]{0:T(256)S(1)} %dynamic_slice.18) | copy-start | bytes 3076
  29.6 83.0 %copy-start.10 = (s32[256]{0:T(256)}, s32[256]{0:T(256)S(1)}, u32[]{:S(2)}) copy-start(s32[256]{0:T(256)S(1)} %iota_add_fusion.1) | copy-start | bytes 3076
  100.7 3.6 %copy-start.11 = (bf16[1024,4096]{1,0:T(8,128)(2,1)}, bf16[1024,4096]{1,0:T(8,128)(2,1)S(1)}, u32[]{:S(2)}) copy-start(bf16[1024,4096]{1,0:T(8,128)(2,1)S(1)} %convert_bitcast_fusion) | copy-start | bytes 25165828
  100.7 3.6 %copy-start.4 = (f32[128,128]{1,0:T(8,128)S(1)}, f32[128,128]{1,0:T(8,128)}, u32[]{:S(2)}) copy-start(f32[128,128]{1,0:T(8,128)} %get-tuple-element.10) | copy-start | bytes 196612
  104.3 2.0 %copy-start.3 = (f32[4096,256]{1,0:T(8,128)}, f32[4096,256]{1,0:T(8,128)S(1)}, u32[]{:S(2)}) copy-start(f32[4096,256]{1,0:T(8,128)S(1)} %convolution_add_fusion) | copy-start | bytes 12582916
  104.3 2.2 %copy-start.8 = (f32[128,128]{1,0:T(8,128)S(1)}, f32[128,128]{1,0:T(8,128)}, u32[]{:S(2)}) copy-start(f32[128,128]{1,0:T(8,128)} %get-tuple-element.9) | copy-start | bytes 196612
  106.4 2.5 %copy-start.7 = (f32[128,128]{1,0:T(8,128)S(1)}, f32[128,128]{1,0:T(8,128)}, u32[]{:S(2)}) copy-start(f32[128,128]{1,0:T(8,128)} %get-tuple-element.12) | copy-start | bytes 196612
  108.7 2.8 %copy-start.2 = (bf16[64,256,128]{2,1,0:T(8,128)(2,1)S(1)}, bf16[64,256,128]{2,1,0:T(8,128)(2,1)}, u32[]{:S(2)}) copy-start(bf16[64,256,128]{2,1,0:T(8,128)(2,1)} %all-gather.2.cloned.1.call-done) | copy-start | bytes 12582916
  110.7 2.3 %copy-start.1 = (bf16[4096,128]{1,0:T(8,128)(2,1)}, bf16[4096,128]{1,0:T(8,128)(2,1)S(1)}, u32[]{:S(2)}) copy-start(bf16[4096,128]{1,0:T(8,128)(2,1)S(1)} %fusion.49) | copy-start | bytes 3145732
  111.4 2.1 %copy-start.6 = (f32[128,128]{1,0:T(8,128)S(1)}, f32[128,128]{1,0:T(8,128)}, u32[]{:S(2)}) copy-start(f32[128,128]{1,0:T(8,128)} %get-tuple-element.11) | copy-start | bytes 196612
  112.6 1.2 copy-start.5
  113.3 3.6 %slice-start = ((bf16[4096,128]{1,0:T(8,128)(2,1)}), bf16[3840,128]{1,0:T(8,128)(2,1)S(1)}, s32[]{:S(2)}) async-start(bf16[4096,128]{1,0:T(8,128)(2,1)} %copy-done.1), calls=%async_computation.2 | async-start | bytes 1966080 | tf_op jit(solution)/shard_map/slice | solution.py:116
Sparse Core Ops, SparseCore 0:
  10.1 85.5 all-gather.1
